TPU v7x, 32 devices: a whole 2x2x4 slice. The times are simulated.
32 devices in a mesh: dp: 8 (over z, x), mp: 4 (over y, core).
Axes of the slice: x: 2, y: 2, z: 4, core: 2. Of those that a mesh axis runs over, the one named last changes fastest.
Arguments:
- queries: bfloat16 [1024, 4, 8192], P('dp', None, 'mp'), may hold values from -6 to 6
- fresh_key_value: bfloat16 [1024, 4, 2, 8, 128], P('dp', None, None, 'mp'), may hold values from -6 to 6
- key_value_pool: bfloat16 [4096, 2, 8, 16, 128], P('dp', None, 'mp'), may hold values from -6 to 6
- block_position_map: int32 [4096], replicated, may hold values from 0 to 4095
- request_blocks: int32 [1024, 4], P('dp'), may hold values from 0 to 4095, as said below
- live_prefix_length: int32 [1024], P('dp'), may hold values from 1 to 64, as said below
- request_adapter: int32 [1024, 1], P('dp'), may hold values from 0 to 15; in each aligned block of 128 rows (0 to 127, 128 to 255, ...) at most 8 rows name the same one
- output_weight: bfloat16 [8192, 8192], P('mp'), may hold values from -0.0625 to 0.0625
- adapter_down_panels: bfloat16 [16, 64, 8192], P('dp', None, 'mp'), may hold values from -0.0625 to 0.0625
- adapter_up_panels: bfloat16 [16, 64, 8192], P('dp', None, 'mp'), may hold values from -0.75 to 0.75
Outputs:
- layer_out: bfloat16 [1024, 4, 8192], P('dp', None, 'mp')
Inputs may be any that keep to these rules, and one draw needn't show every extreme that they name: `request_blocks`: every logical block is given a distinct pool position. The 512 entries of one index of dp name 256 distinct blocks, each exactly twice. Through the owner map at most 64 distinct blocks of one index of dp, and so at most 128 of its entries, lie on one pool owner (pool positions owner * 512 to owner * 512 + 511); one pool owner holds exactly 64 distinct blocks of every index of dp. `live_prefix_length`: all requests of some index of dp have the full 4 * 16 prefix tokens. `request_adapter`: among the 128 requests of one index of dp no adapter appears more than 8 times, and that many is reached.
All inputs are finite; a program needn't handle non-finite values.
Results may differ from a plain program's by a relative error of at most 0.008.
Values may be sent and summed in bfloat16 or wider, within the bound.
No kernel may reach another device: no remote copies, remote signals or barrier semaphores. Data moves between devices by JAX's collectives and lax.ppermute only.
A program may use at most 192 MiB of HBM per device.

v0:
```python
import jax
import jax.numpy as jnp
from jax import lax
from jax.sharding import PartitionSpec as P

ADAPTER_SCALE = 2.0


def shards(
    queries,
    fresh_key_value,
    key_value_pool,
    block_position_map,
    request_blocks,
    live_prefix_length,
    request_adapter,
    output_weight,
    adapter_down_panels,
    adapter_up_panels,
):
    owners = lax.axis_size("dp")
    req_dev, step_count, query_width = queries.shape
    kv_heads = fresh_key_value.shape[3]
    head_dim = fresh_key_value.shape[4]
    pool_dev = key_value_pool.shape[0]
    block_len = key_value_pool.shape[3]
    blocks_per = request_blocks.shape[1]
    entries = req_dev * blocks_per
    out_width = output_weight.shape[1]
    owner_range = jnp.arange(owners)
    positions = jnp.take(block_position_map, request_blocks.reshape(entries))
    target = positions // pool_dev
    local_slot = positions % pool_dev
    capacity = entries // owners
    entry_ids = jnp.arange(entries)
    same_block = positions[:, None] == positions[None, :]
    earlier = entry_ids[None, :] < entry_ids[:, None]
    first = jnp.logical_not(jnp.any(same_block & earlier, axis=1))
    same_owner = target[:, None] == target[None, :]
    rank = jnp.sum((same_owner & earlier & first[None, :]).astype(jnp.int32), axis=1)
    first_of = same_block & first[None, :]
    slot_index = jnp.sum(jnp.where(first_of, rank[None, :], 0), axis=1)
    key = jnp.where(first, target * capacity + rank, -1)
    table_ids = jnp.arange(owners * capacity)
    wish_table = jnp.sum(
        jnp.where(key[:, None] == table_ids[None, :], local_slot[:, None], 0), axis=0
    ).reshape(owners, capacity)
    wanted = lax.all_to_all(wish_table, "dp", split_axis=0, concat_axis=0, tiled=True)
    served = jnp.take(key_value_pool, wanted.reshape(-1), axis=0).reshape(
        (owners, capacity) + key_value_pool.shape[1:]
    )
    fetched = lax.all_to_all(served, "dp", split_axis=0, concat_axis=0, tiled=True)
    flat_rows = fetched.reshape((owners * capacity,) + key_value_pool.shape[1:])
    own_blocks = jnp.take(flat_rows, target * capacity + slot_index, axis=0)
    own_blocks = own_blocks.reshape((req_dev, blocks_per) + key_value_pool.shape[1:])
    group_size = query_width // (kv_heads * head_dim)
    query = queries.reshape(req_dev, step_count, kv_heads, group_size, head_dim)
    score_scale = head_dim ** (-0.5)
    prefix_scores = (
        jnp.einsum(
            "qsghd,qbgtd->qsghbt", query, own_blocks[:, :, 0], preferred_element_type=jnp.float32
        )
        * score_scale
    )
    token_index = jnp.arange(blocks_per)[:, None] * block_len + jnp.arange(block_len)[None, :]
    live_mask = token_index[None] < live_prefix_length[:, None, None]
    prefix_scores = jnp.where(live_mask[:, None, None, None], prefix_scores, -jnp.inf)
    fresh_scores = (
        jnp.einsum(
            "qsghd,qjgd->qsghj", query, fresh_key_value[:, :, 0], preferred_element_type=jnp.float32
        )
        * score_scale
    )
    causal = jnp.arange(step_count)[None, :] <= jnp.arange(step_count)[:, None]
    fresh_scores = jnp.where(causal[None, :, None, None, :], fresh_scores, -jnp.inf)
    row_top = jnp.maximum(jnp.max(prefix_scores, axis=(4, 5)), jnp.max(fresh_scores, axis=4))
    prefix_w = jnp.exp(prefix_scores - row_top[..., None, None])
    fresh_w = jnp.exp(fresh_scores - row_top[..., None])
    row_total = jnp.sum(prefix_w, axis=(4, 5)) + jnp.sum(fresh_w, axis=4)
    prefix_p = (prefix_w / row_total[..., None, None]).astype(jnp.bfloat16)
    fresh_p = (fresh_w / row_total[..., None]).astype(jnp.bfloat16)
    attended = jnp.einsum(
        "qsghbt,qbgtd->qsghd", prefix_p, own_blocks[:, :, 1], preferred_element_type=jnp.float32
    )
    attended = attended + jnp.einsum(
        "qsghj,qjgd->qsghd", fresh_p, fresh_key_value[:, :, 1], preferred_element_type=jnp.float32
    )
    attended = attended.astype(jnp.bfloat16).reshape(req_dev, step_count, query_width)
    base_product = jnp.dot(
        attended.reshape(req_dev * step_count, query_width),
        output_weight,
        preferred_element_type=jnp.float32,
    )
    base_product = base_product.reshape(req_dev, step_count, out_width)
    adapter = request_adapter[:, 0]
    single_panel = lax.all_gather(adapter_down_panels, "dp", axis=0, tiled=True)
    panel_count = single_panel.shape[0]
    hit_mask = (adapter[:, None] == jnp.arange(panel_count)[None, :]).astype(jnp.float32)
    every_rank = jnp.einsum(
        "qsf,nrf->qsnr", attended, single_panel, preferred_element_type=jnp.float32
    )
    rank_part = jnp.einsum("qsnr,qn->qsr", every_rank, hit_mask)
    rank_sum = lax.psum(rank_part, "mp").astype(jnp.bfloat16)
    single_panel = lax.all_gather(adapter_up_panels, "dp", axis=0, tiled=True)
    panel_count = single_panel.shape[0]
    hit_mask = (adapter[:, None] == jnp.arange(panel_count)[None, :]).astype(jnp.bfloat16)
    selected_panel = rank_sum[:, :, None, :] * hit_mask[:, None, :, None]
    adapter_sum = jnp.einsum(
        "utja,jam->utm", selected_panel, single_panel, preferred_element_type=jnp.float32
    )
    adapter_output = (adapter_sum * ADAPTER_SCALE).astype(jnp.bfloat16)
    summed_output = lax.psum_scatter(base_product, "mp", scatter_dimension=2, tiled=True)
    return (summed_output + adapter_output.astype(jnp.float32)).astype(jnp.bfloat16)


def solution(mesh):
    in_specs = (
        P("dp", None, "mp"),
        P("dp", None, None, "mp", None),
        P("dp", None, "mp", None, None),
        P(),
        P("dp", None),
        P("dp"),
        P("dp", None),
        P("mp", None),
        P("dp", None, "mp"),
        P("dp", None, "mp"),
    )
    out_specs = P("dp", None, "mp")
    return jax.shard_map(shards, mesh=mesh, in_specs=in_specs, out_specs=out_specs, check_vma=False)
```

profile of v0, /device:TPU:0, one launch (start us, length us, event | category | flops | bytes accessed | tf_op | source)
XLA Modules:
  0.0 584.8 jit_solution(10500240088412221773)
XLA Ops:
  8.4 3.1 gather_fusion
  12.4 13.5 %all_to_all.14 = s32[8,1,64]{2,1,0:T(1,128)S(1)} all-to-all(s32[8,1,64]{2,1,0:T(1,128)S(1)} %all_to_all.9), channel_id=1, replica_groups=mesh['dp'=8,'mp'=4] {'dp'}, dimensions={0} | all-to-all | bytes 4096 | tf_op jit(solution)/shard_map/all_to_all | solution.py:48
  27.2 22.9 %gather_fusion.1 = bf16[512,2,2,16,128]{4,3,2,1,0:T(8,128)(2,1)} fusion(bf16[512,2,2,16,128]{4,3,2,1,0:T(8,128)(2,1)} %param.14, s32[1024]{0:T(1024)S(1)} %pad_clamp_fusion.1), kind=kCustom, calls=%fused_computation.clone | custom fusion | bytes 16779264 | tf_op jit(solution)/shard_map/jit(_take)/gather | solution.py:49
  50.1 7.6 %broadcast_select_fusion.1 = bf16[512,2,2,16,128]{4,3,2,1,0:T(8,128)(2,1)} fusion(bf16[512,2,2,16,128]{4,3,2,1,0:T(8,128)(2,1)} %gather_fusion.1, pred[512]{0:T(512)(128)(4,1)S(1)} %compare_and_fusion.3), kind=kLoop, calls=%fused_computation.6 | loop fusion | flops 4194304 | bytes 16777728 | tf_op jit(solution)/shard_map/jit(_take)/select_n | solution.py:49
  57.7 5.0 all-to-all-start.1
  64.4 3.2 reshape.275
  68.0 10.8 %fusion.37 = (f32[128,4,2,8]{3,1,2,0:T(4,128)S(1)}, f32[128,4,2,8,4]{3,4,1,2,0:T(4,128)}) fusion(bf16[128,4,2,8,128]{4,3,2,1,0:T(8,128)(2,1)S(1)} %reshape.275, bf16[128,4,1,2,128]{4,3,2,1,0:T(2,128)(2,1)S(1)} %get-tuple-element.13, pred[4,4]{1,0:T(4,128)(4,1)S(1)} %iota_compare_fusion.3), kind=kOutput, calls=%fused_computation.79 | convolution fusion | flops 8478720 | bytes 2523152 | tf_op jit(solution)/shard_map/qsghd,qjgd->qsghj/dot_general | solution.py:69
  79.5 232.6 %all-to-all-done.1 = bf16[8,64,2,2,16,128]{5,4,3,2,1,0:T(8,128)(2,1)} async-done(((bf16[8,64,2,2,16,128]{5,4,3,2,1,0:T(8,128)(2,1)}), bf16[8,64,2,2,16,128]{5,4,3,2,1,0:T(8,128)(2,1)}, u32[]{:S(2)}, u32[]{:S(2)}) %all-to-all-start.1) | async-done | bytes 8388640 | tf_op jit(solution)/shard_map/all_to_all | solution.py:52
  312.1 23.6 %gather_fusion.2 = bf16[512,2,2,16,128]{4,3,2,1,0:T(8,128)(2,1)} fusion(bf16[512,2,2,16,128]{4,3,2,1,0:T(8,128)(2,1)} %bitcast.3, s32[1024]{0:T(1024)S(1)} %pad_clamp_fusion), kind=kCustom, calls=%fused_computation.1.clone | custom fusion | bytes 16779264 | tf_op jit(solution)/shard_map/jit(_take)/gather | solution.py:54
  335.7 4.9 broadcast_select_fusion
  340.6 3.7 fusion.35
  344.3 17.3 %fusion.2 = f32[128,2,4,16,4,8]{3,5,4,2,1,0:T(8,128)} fusion(bf16[128,4,1,2,16,128]{5,4,3,2,1,0:T(8,128)(2,1)S(1)} %get-tuple-element.11, bf16[128,4,2,8,128]{4,3,2,1,0:T(8,128)(2,1)S(1)} %reshape.275), kind=kOutput, calls=%fused_computation.8 | convolution fusion | flops 134217728 | bytes 8388608 | tf_op jit(solution)/shard_map/qsghd,qbgtd->qsghbt/dot_general | solution.py:60
  361.6 12.2 %copy.92 = f32[128,2,4,16,4,8]{0,3,2,5,1,4:T(8,128)S(1)} copy(f32[128,2,4,16,4,8]{3,5,4,2,1,0:T(8,128)} %fusion.2) | data formatting | bytes 4194304 | tf_op jit(solution)/shard_map/qsghd,qbgtd->qsghbt/dot_general | solution.py:60
  374.5 3.6 fusion.22
  380.6 22.9 %copy.98 = bf16[128,4,2,8,4,16]{5,3,4,1,2,0:T(8,128)(2,1)} copy(bf16[128,4,2,8,4,16]{0,5,4,3,2,1:T(8,128)(2,1)S(1)} %divide_convert_fusion) | data formatting | bytes 2097152 | tf_op jit(solution)/shard_map/convert_element_type | solution.py:80
  403.5 7.0 %fusion.3 = f32[128,2,128,4,8,1]{2,4,5,3,1,0:T(8,128)S(1)} fusion(bf16[128,4,2,8,4,16]{5,3,4,1,2,0:T(8,128)(2,1)} %copy.98, bf16[128,4,1,2,16,128]{5,4,3,2,1,0:T(8,128)(2,1)} %get-tuple-element.10), kind=kOutput, calls=%fused_computation.10 | convolution fusion | flops 134217728 | bytes 9437184 | tf_op jit(solution)/shard_map/qsghbt,qbgtd->qsghd/dot_general | solution.py:82
  410.5 2.6 fusion.4
  413.1 3.4 copy.101
  416.6 27.0 %fusion = f32[128,4,8192]{2,0,1:T(8,128)} fusion(bf16[128,4,2048]{0,2,1:T(8,128)(2,1)S(1)} %bitcast.89, bf16[2048,8192]{1,0:T(8,128)(2,1)} %param.19), kind=kOutput, calls=%fused_computation.3 | convolution fusion | flops 17179869184 | bytes 52428800 | tf_op jit(solution)/shard_map/dot_general | solution.py:89
  444.2 4.5 multiply_reduce_fusion
  448.7 11.7 %all-reduce.1 = bf16[128,4,64]{0,2,1:T(8,128)(2,1)S(1)} all-reduce(f32[128,4,64]{0,2,1:T(8,128)S(1)} %multiply_reduce_fusion), channel_id=1, replica_groups=mesh['dp'=8,'mp'=4] {'mp'}, use_global_device_ids=true, to_apply=%region_9.11 | all-reduce | flops 32768 | bytes 196608 | tf_op jit(solution)/shard_map/psum | solution.py:103
  460.5 107.8 %reduce-scatter.2.cloned.1.call-done = f32[128,4,2048]{2,0,1:T(8,128)} async-done(((f32[128,4,8192]{2,0,1:T(8,128)}), f32[128,4,2048]{2,0,1:T(8,128)}) %reduce-scatter.2.cloned.1.call-update) | async-done | bytes 4194320 | tf_op jit(solution)/shard_map/reduce_scatter | solution.py:112
  568.3 5.9 %add_convert_fusion = bf16[128,4,2048]{2,0,1:T(8,128)(2,1)S(1)} fusion(f32[128,4,2048]{2,0,1:T(8,128)} %reduce-scatter.2.cloned.1.call-done, bf16[16,64,2048]{2,1,0:T(8,128)(2,1)} %all-gather.5.cloned.1.call-done, bf16[128,16]{0,1:T(8,128)(2,1)S(1)} %get-tuple-element.15, bf16[128,4,64]{0,2,1:T(8,128)(2,1)S(1)} %all-reduce.1), kind=kOutput, calls=%fused_computation.19 | convolution fusion | flops 2153250816 | bytes 10555392 | tf_op jit(solution)/shard_map/utja,jam->utm/dot_general | solution.py:108
  574.2 2.9 copy.104
  (62 shorter events, 9.7 us)
Async XLA Ops:
  7.4 1.0 copy-start
  57.7 254.4 %all-to-all-start.1 = ((bf16[8,64,2,2,16,128]{5,4,3,2,1,0:T(8,128)(2,1)}), bf16[8,64,2,2,16,128]{5,4,3,2,1,0:T(8,128)(2,1)}, u32[]{:S(2)}, u32[]{:S(2)}) async-start(bf16[8,64,2,2,16,128]{5,4,3,2,1,0:T(8,128)(2,1)} %bitcast.87), calls=%async_computation.1 | async-start | bytes 16777216 | tf_op jit(solution)/shard_map/all_to_all | solution.py:52
  62.7 381.5 %all-gather.3.cloned.1.call-start = ((), (), s32[]{:S(2)}) async-start(), calls=%async_computation.4 | async-start | bytes 4718592 | tf_op jit(solution)/shard_map/all_gather | solution.py:96
  63.4 397.0 %all-gather.5.cloned.1.call-start = ((), (), s32[]{:S(2)}) async-start(), calls=%async_computation.5 | async-start | bytes 4718592 | tf_op jit(solution)/shard_map/all_gather | solution.py:104
  64.2 3.4 copy-start.5
  64.2 504.1 %reduce-scatter.2.cloned.1.call-start = ((), (), s32[]{:S(2)}) async-start(), calls=%async_computation.3 | async-start | bytes 20971520 | tf_op jit(solution)/shard_map/reduce_scatter | solution.py:112
  68.0 11.5 %copy-start.8 = (s32[128]{0:T(128)S(1)}, s32[128]{0:T(128)}, u32[]{:S(2)}) copy-start(s32[128]{0:T(128)} %param.17) | copy-start | bytes 1540
  374.5 4.4 copy-start.3
  403.4 7.0 %copy-start.2 = (f32[128,4,2,8,4]{3,4,1,2,0:T(4,128)S(1)}, f32[128,4,2,8,4]{3,4,1,2,0:T(4,128)}, u32[]{:S(2)}) copy-start(f32[128,4,2,8,4]{3,4,1,2,0:T(4,128)} %get-tuple-element.17) | copy-start | bytes 393220
  403.4 7.0 %copy-start.4 = (f32[128,4,2,8]{3,1,2,0:T(4,128)S(1)}, f32[128,4,2,8]{3,1,2,0:T(4,128)}, u32[]{:S(2)}) copy-start(f32[128,4,2,8]{3,1,2,0:T(4,128)} %copy-done.3) | copy-start | bytes 98308
  403.5 7.0 %copy-start.6 = (f32[128,4,2,8]{3,1,2,0:T(4,128)S(1)}, f32[128,4,2,8]{3,1,2,0:T(4,128)}, u32[]{:S(2)}) copy-start(f32[128,4,2,8]{3,1,2,0:T(4,128)} %copy.99) | copy-start | bytes 98308
  443.5 0.7 copy-start.7
  568.3 8.8 %copy-start.1 = (s32[4096]{0:T(1024)S(1)}, s32[4096]{0:T(1024)}, u32[]{:S(2)}) copy-start(s32[4096]{0:T(1024)} %param.15) | copy-start | bytes 49156
Sparse Core Ops, SparseCore 0:
  65.9 202.7 all-gather.2
  271.0 83.5 all-gather.4
Sparse Core Ops, SparseCore 1:
  443.7 124.6 reduce-scatter.1
where the time goes:
time: 592 us; the launch traced here: 585 us
  waiting for transfers between devices  342 us (58%)
  local copies, waits for them, and re-layouts  102 us (17%)
  matrix products  75.1 us (13%)
  blocking collectives  25.2 us (4%)
  other arithmetic  19.7 us (3%)
  between operations  15.4 us (3%)
    all_to_all x1, waiting for transfers between devices, shards(): lax.all_to_all(served, 'dp', split_axis=0, concat_axis=0, tiled=True)  233 us
    reduce_scatter x1, waiting for transfers between devices, shards(): lax.psum_scatter(base_product, 'mp', scatter_dimension=2, tiled=True)  108 us
    dot_general x1, matrix products, shards(): jnp.dot(attended.reshape(req_dev * step_count, query_width), output_weigh...  27 us
    gather x1, local copies, waits for them, and re-layouts, shards(): own_blocks = jnp.take(flat_rows, target * capacity + slot_index, axis=0)  23.6 us
    gather x1, local copies, waits for them, and re-layouts, shards(): jnp.take(key_value_pool, wanted.reshape(-1), axis=0)  22.9 us
    convert_element_type x1, local copies, waits for them, and re-layouts, shards(): prefix_p = (prefix_w / row_total[..., None, None]).astype(jnp.bfloat16)  22.9 us
    dot_general x1, matrix products, shards(): jnp.einsum('qsghd,qbgtd->qsghbt', query, own_blocks[:, :, 0], preferred_e...  17.3 us
    all_to_all x1, blocking collectives, shards(): lax.all_to_all(wish_table, 'dp', split_axis=0, concat_axis=0, tiled=True)  13.5 us
  transfers between devices with their start and end apart: 4, of which 2 were waited for; matrix products, arithmetic and copies ran while one was open for 26% of the time, Pallas kernels for 0%

commit v1 on v0

--- a/solution.py
+++ b/solution.py
@@ -45,7 +45,18 @@
     wish_table = jnp.sum(
         jnp.where(key[:, None] == table_ids[None, :], local_slot[:, None], 0), axis=0
     ).reshape(owners, capacity)
-    wanted = lax.all_to_all(wish_table, "dp", split_axis=0, concat_axis=0, tiled=True)
+    ways, here = (lax.axis_size("dp"), lax.axis_index("dp"))
+    width = wish_table.shape[0] // ways
+    dims = list(wish_table.shape)
+    dims[0] = width
+    height = dims[0]
+    dims[0] = height * ways
+    wanted = jnp.zeros(dims, wish_table.dtype)
+    for mask in range(ways):
+        part = lax.dynamic_slice_in_dim(wish_table, (here ^ mask) * width, width, axis=0)
+        if mask:
+            part = lax.ppermute(part, "dp", [(d, d ^ mask) for d in range(ways)])
+        wanted = lax.dynamic_update_slice_in_dim(wanted, part, (here ^ mask) * height, axis=0)
     served = jnp.take(key_value_pool, wanted.reshape(-1), axis=0).reshape(
         (owners, capacity) + key_value_pool.shape[1:]
     )

time: 592 us -> 595 us (level)
  blocking collectives: 25.2 us -> 11.7 us
  starting transfers between devices: 5.26 us -> 17.8 us
    all_to_all x1 -> x0, blocking collectives: 13.5 us -> none  [shards(): lax.all_to_all(wish_table, 'dp', split_axis=0, concat_axis=0, tiled=True)]
    ppermute x0 -> x7, starting transfers between devices: none -> 12.6 us  [shards(): part = lax.ppermute(part, 'dp', [(d, d ^ mask) for d in range(ways)])]
    ppermute x0 -> x7, waiting for transfers between devices: none -> 6.05 us  [shards(): part = lax.ppermute(part, 'dp', [(d, d ^ mask) for d in range(ways)])]
  transfers between devices with their start and end apart: 4 -> 11, of which waited for: 2 -> 5; matrix products, arithmetic and copies ran while one was open for 26% -> 26% of each run, Pallas kernels for 0% -> 0%
where the time goes in v1:
time: 595 us; the launch traced here: 588 us
  waiting for transfers between devices  346 us (58%)
  local copies, waits for them, and re-layouts  102 us (17%)
  matrix products  75.3 us (13%)
  other arithmetic  19.1 us (3%)
  starting transfers between devices  17.8 us (3%)
  between operations  15.4 us (3%)
  blocking collectives  11.7 us (2%)
    all_to_all x1, waiting for transfers between devices, shards(): lax.all_to_all(served, 'dp', split_axis=0, concat_axis=0, tiled=True)  231 us
    reduce_scatter x1, waiting for transfers between devices, shards(): lax.psum_scatter(base_product, 'mp', scatter_dimension=2, tiled=True)  108 us
    dot_general x1, matrix products, shards(): jnp.dot(attended.reshape(req_dev * step_count, query_width), output_weigh...  27 us
    gather x1, local copies, waits for them, and re-layouts, shards(): own_blocks = jnp.take(flat_rows, target * capacity + slot_index, axis=0)  23.6 us
    gather x1, local copies, waits for them, and re-layouts, shards(): jnp.take(key_value_pool, wanted.reshape(-1), axis=0)  22.9 us
    convert_element_type x1, local copies, waits for them, and re-layouts, shards(): prefix_p = (prefix_w / row_total[..., None, None]).astype(jnp.bfloat16)  22.9 us
    dot_general x1, matrix products, shards(): jnp.einsum('qsghd,qbgtd->qsghbt', query, own_blocks[:, :, 0], preferred_e...  17.3 us
    ppermute x7, starting transfers between devices, shards(): part = lax.ppermute(part, 'dp', [(d, d ^ mask) for d in range(ways)])  12.6 us
  transfers between devices with their start and end apart: 11, of which 5 were waited for; matrix products, arithmetic and copies ran while one was open for 26% of the time, Pallas kernels for 0%

profile of v1, /device:TPU:0, one launch (start us, length us, event | category | flops | bytes accessed | tf_op | source)
XLA Modules:
  0.0 587.7 jit_solution(1663309792171998617)
XLA Ops:
  8.5 3.1 gather_fusion
  17.1 3.0 collective-permute-start.3
  21.4 3.7 collective-permute-start.5
  26.8 4.6 collective-permute-done.6
  31.5 22.9 %gather_fusion.1 = bf16[512,2,2,16,128]{4,3,2,1,0:T(8,128)(2,1)} fusion(bf16[512,2,2,16,128]{4,3,2,1,0:T(8,128)(2,1)} %param.14, s32[1024]{0:T(1024)S(1)} %pad_clamp_fusion.1), kind=kCustom, calls=%fused_computation.clone | custom fusion | bytes 16779264 | tf_op jit(solution)/shard_map/jit(_take)/gather | solution.py:60
  54.4 7.6 %broadcast_select_fusion.1 = bf16[512,2,2,16,128]{4,3,2,1,0:T(8,128)(2,1)} fusion(bf16[512,2,2,16,128]{4,3,2,1,0:T(8,128)(2,1)} %gather_fusion.1, pred[512]{0:T(512)(128)(4,1)S(1)} %compare_and_fusion.3), kind=kLoop, calls=%fused_computation.6 | loop fusion | flops 4194304 | bytes 16777728 | tf_op jit(solution)/shard_map/jit(_take)/select_n | solution.py:60
  62.0 4.9 all-to-all-start
  68.7 3.2 reshape.274
  72.2 10.8 %fusion.37 = (f32[128,4,2,8]{3,1,2,0:T(4,128)S(1)}, f32[128,4,2,8,4]{3,4,1,2,0:T(4,128)}) fusion(bf16[128,4,2,8,128]{4,3,2,1,0:T(8,128)(2,1)S(1)} %reshape.274, bf16[128,4,1,2,128]{4,3,2,1,0:T(2,128)(2,1)S(1)} %get-tuple-element.13, pred[4,4]{1,0:T(4,128)(4,1)S(1)} %iota_compare_fusion.3), kind=kOutput, calls=%fused_computation.87 | convolution fusion | flops 8478720 | bytes 2523152 | tf_op jit(solution)/shard_map/qsghd,qjgd->qsghj/dot_general | solution.py:80
  83.8 231.2 %all-to-all-done = bf16[8,64,2,2,16,128]{5,4,3,2,1,0:T(8,128)(2,1)} async-done(((bf16[8,64,2,2,16,128]{5,4,3,2,1,0:T(8,128)(2,1)}), bf16[8,64,2,2,16,128]{5,4,3,2,1,0:T(8,128)(2,1)}, u32[]{:S(2)}, u32[]{:S(2)}) %all-to-all-start) | async-done | bytes 8388640 | tf_op jit(solution)/shard_map/all_to_all | solution.py:63
  314.9 23.6 %gather_fusion.2 = bf16[512,2,2,16,128]{4,3,2,1,0:T(8,128)(2,1)} fusion(bf16[512,2,2,16,128]{4,3,2,1,0:T(8,128)(2,1)} %bitcast.3, s32[1024]{0:T(1024)S(1)} %pad_clamp_fusion), kind=kCustom, calls=%fused_computation.1.clone | custom fusion | bytes 16779264 | tf_op jit(solution)/shard_map/jit(_take)/gather | solution.py:65
  338.6 4.9 broadcast_select_fusion
  343.5 3.7 fusion.35
  347.2 17.3 %fusion.2 = f32[128,2,4,16,4,8]{3,5,4,2,1,0:T(8,128)} fusion(bf16[128,4,1,2,16,128]{5,4,3,2,1,0:T(8,128)(2,1)S(1)} %get-tuple-element.11, bf16[128,4,2,8,128]{4,3,2,1,0:T(8,128)(2,1)S(1)} %reshape.274), kind=kOutput, calls=%fused_computation.8 | convolution fusion | flops 134217728 | bytes 8388608 | tf_op jit(solution)/shard_map/qsghd,qbgtd->qsghbt/dot_general | solution.py:71
  364.5 12.2 %copy.92 = f32[128,2,4,16,4,8]{0,3,2,5,1,4:T(8,128)S(1)} copy(f32[128,2,4,16,4,8]{3,5,4,2,1,0:T(8,128)} %fusion.2) | data formatting | bytes 4194304 | tf_op jit(solution)/shard_map/qsghd,qbgtd->qsghbt/dot_general | solution.py:71
  377.3 3.6 fusion.22
  383.4 22.9 %copy.98 = bf16[128,4,2,8,4,16]{5,3,4,1,2,0:T(8,128)(2,1)} copy(bf16[128,4,2,8,4,16]{0,5,4,3,2,1:T(8,128)(2,1)S(1)} %divide_convert_fusion) | data formatting | bytes 2097152 | tf_op jit(solution)/shard_map/convert_element_type | solution.py:91
  406.3 7.0 %fusion.3 = f32[128,2,128,4,8,1]{2,4,5,3,1,0:T(8,128)S(1)} fusion(bf16[128,4,2,8,4,16]{5,3,4,1,2,0:T(8,128)(2,1)} %copy.98, bf16[128,4,1,2,16,128]{5,4,3,2,1,0:T(8,128)(2,1)} %get-tuple-element.10), kind=kOutput, calls=%fused_computation.10 | convolution fusion | flops 134217728 | bytes 9437184 | tf_op jit(solution)/shard_map/qsghbt,qbgtd->qsghd/dot_general | solution.py:93
  416.0 3.4 copy.101
  419.4 27.0 %fusion = f32[128,4,8192]{2,0,1:T(8,128)} fusion(bf16[128,4,2048]{0,2,1:T(8,128)(2,1)S(1)} %bitcast.89, bf16[2048,8192]{1,0:T(8,128)(2,1)} %param.19), kind=kOutput, calls=%fused_computation.3 | convolution fusion | flops 17179869184 | bytes 52428800 | tf_op jit(solution)/shard_map/dot_general | solution.py:100
  447.2 4.5 multiply_reduce_fusion
  451.7 11.7 %all-reduce.1 = bf16[128,4,64]{0,2,1:T(8,128)(2,1)S(1)} all-reduce(f32[128,4,64]{0,2,1:T(8,128)S(1)} %multiply_reduce_fusion), channel_id=1, replica_groups=mesh['dp'=8,'mp'=4] {'mp'}, use_global_device_ids=true, to_apply=%region_9.11 | all-reduce | flops 32768 | bytes 196608 | tf_op jit(solution)/shard_map/psum | solution.py:114
  463.4 107.8 %reduce-scatter.2.cloned.1.call-done = f32[128,4,2048]{2,0,1:T(8,128)} async-done(((f32[128,4,8192]{2,0,1:T(8,128)}), f32[128,4,2048]{2,0,1:T(8,128)}) %reduce-scatter.2.cloned.1.call-update) | async-done | bytes 4194320 | tf_op jit(solution)/shard_map/reduce_scatter | solution.py:123
  571.2 5.9 add_convert_fusion
  (83 shorter events, 21.8 us)
Async XLA Ops:
  7.4 1.1 copy-start
  12.5 8.9 %collective-permute-start = (s32[1,64]{1,0:T(1,128)S(1)}, s32[1,64]{1,0:T(1,128)S(1)}, u32[]{:S(2)}, u32[]{:S(2)}) collective-permute-start(s32[1,64]{1,0:T(1,128)S(1)} %get-tuple-element.20), channel_id=1, source_target_pairs={{0,4},{4,0},{8,12},{12,8},{16,20},{20,16},{24,28},{28,24},{1,5},{5... | collective-permute-start | bytes 776 | tf_op jit(solution)/shard_map/ppermute | solution.py:58
  15.5 9.6 %collective-permute-start.1 = (s32[1,64]{1,0:T(1,128)S(1)}, s32[1,64]{1,0:T(1,128)S(1)}, u32[]{:S(2)}, u32[]{:S(2)}) collective-permute-start(s32[1,64]{1,0:T(1,128)S(1)} %get-tuple-element.19), channel_id=1, source_target_pairs={{0,8},{4,12},{8,0},{12,4},{16,24},{20,28},{24,16},{28,20},{1,9},{5... | collective-permute-start | bytes 776 | tf_op jit(solution)/shard_map/ppermute | solution.py:58
  17.1 8.1 %collective-permute-start.2 = (s32[1,64]{1,0:T(1,128)S(1)}, s32[1,64]{1,0:T(1,128)S(1)}, u32[]{:S(2)}, u32[]{:S(2)}) collective-permute-start(s32[1,64]{1,0:T(1,128)S(1)} %get-tuple-element.18), channel_id=1, source_target_pairs={{0,12},{4,8},{8,4},{12,0},{16,28},{20,24},{24,20},{28,16},{1,13},{... | collective-permute-start | bytes 776 | tf_op jit(solution)/shard_map/ppermute | solution.py:58
  17.1 8.2 %collective-permute-start.3 = (s32[1,64]{1,0:T(1,128)S(1)}, s32[1,64]{1,0:T(1,128)S(1)}, u32[]{:S(2)}, u32[]{:S(2)}) collective-permute-start(s32[1,64]{1,0:T(1,128)S(1)} %get-tuple-element.17), channel_id=1, source_target_pairs={{0,16},{4,20},{8,24},{12,28},{16,0},{20,4},{24,8},{28,12},{1,17},{... | collective-permute-start | bytes 776 | tf_op jit(solution)/shard_map/ppermute | solution.py:58
  20.1 5.3 collective-permute-start.4
  21.4 5.4 collective-permute-start.5
  25.1 6.3 %collective-permute-start.6 = (s32[1,64]{1,0:T(1,128)S(1)}, s32[1,64]{1,0:T(1,128)S(1)}, u32[]{:S(2)}, u32[]{:S(2)}) collective-permute-start(s32[1,64]{1,0:T(1,128)S(1)} %get-tuple-element.14), channel_id=1, source_target_pairs={{0,28},{4,24},{8,20},{12,16},{16,12},{20,8},{24,4},{28,0},{1,29},{... | collective-permute-start | bytes 776 | tf_op jit(solution)/shard_map/ppermute | solution.py:58
  62.0 253.0 %all-to-all-start = ((bf16[8,64,2,2,16,128]{5,4,3,2,1,0:T(8,128)(2,1)}), bf16[8,64,2,2,16,128]{5,4,3,2,1,0:T(8,128)(2,1)}, u32[]{:S(2)}, u32[]{:S(2)}) async-start(bf16[8,64,2,2,16,128]{5,4,3,2,1,0:T(8,128)(2,1)} %bitcast.87), calls=%async_computation | async-start | bytes 16777216 | tf_op jit(solution)/shard_map/all_to_all | solution.py:63
  66.9 380.2 %all-gather.3.cloned.1.call-start = ((), (), s32[]{:S(2)}) async-start(), calls=%async_computation.3 | async-start | bytes 4718592 | tf_op jit(solution)/shard_map/all_gather | solution.py:107
  67.7 395.7 %all-gather.5.cloned.1.call-start = ((), (), s32[]{:S(2)}) async-start(), calls=%async_computation.4 | async-start | bytes 4718592 | tf_op jit(solution)/shard_map/all_gather | solution.py:115
  68.4 3.4 copy-start.5
  68.4 502.8 %reduce-scatter.2.cloned.1.call-start = ((), (), s32[]{:S(2)}) async-start(), calls=%async_computation.2 | async-start | bytes 20971520 | tf_op jit(solution)/shard_map/reduce_scatter | solution.py:123
  72.2 11.5 %copy-start.8 = (s32[128]{0:T(128)S(1)}, s32[128]{0:T(128)}, u32[]{:S(2)}) copy-start(s32[128]{0:T(128)} %param.17) | copy-start | bytes 1540
  377.3 4.4 copy-start.3
  406.3 7.0 %copy-start.2 = (f32[128,4,2,8,4]{3,4,1,2,0:T(4,128)S(1)}, f32[128,4,2,8,4]{3,4,1,2,0:T(4,128)}, u32[]{:S(2)}) copy-start(f32[128,4,2,8,4]{3,4,1,2,0:T(4,128)} %get-tuple-element.25) | copy-start | bytes 393220
  406.3 7.0 %copy-start.4 = (f32[128,4,2,8]{3,1,2,0:T(4,128)S(1)}, f32[128,4,2,8]{3,1,2,0:T(4,128)}, u32[]{:S(2)}) copy-start(f32[128,4,2,8]{3,1,2,0:T(4,128)} %copy-done.3) | copy-start | bytes 98308
  406.3 7.0 %copy-start.6 = (f32[128,4,2,8]{3,1,2,0:T(4,128)S(1)}, f32[128,4,2,8]{3,1,2,0:T(4,128)}, u32[]{:S(2)}) copy-start(f32[128,4,2,8]{3,1,2,0:T(4,128)} %copy.99) | copy-start | bytes 98308
  446.5 0.7 copy-start.7
  571.2 8.8 %copy-start.1 = (s32[4096]{0:T(1024)S(1)}, s32[4096]{0:T(1024)}, u32[]{:S(2)}) copy-start(s32[4096]{0:T(1024)} %param.15) | copy-start | bytes 49156
Sparse Core Ops, SparseCore 0:
  70.1 201.3 all-gather.2
  273.9 83.5 all-gather.4
Sparse Core Ops, SparseCore 1:
  446.6 124.6 reduce-scatter.1
